TPU v7x, 256 devices: a whole 4x4x8 slice. The times are simulated.
256 devices in a mesh: query: 8 (over x, core), bank: 32 (over z, y).
Axes of the slice: x: 4, y: 4, z: 8, core: 2. Of those that a mesh axis runs over, the one named last changes fastest.
Arguments:
- queries: bfloat16 [2048, 32, 128], P(('query', 'bank'))
- passages: bfloat16 [8192, 128, 128], P('bank')
- passage_home: int32 [8192], replicated, may hold values from 0 to 8191, as said below
- candidates: int32 [2048, 16], P(('query', 'bank')), may hold values from 0 to 8191, as said below
- positive: int32 [2048], P(('query', 'bank')), may hold values from 0 to 15
Outputs:
- losses: float32 [2048], P(('query', 'bank'))
- query_grads: float32 [2048, 32, 128], P(('query', 'bank'))
Inputs may be any that keep to these rules, and one draw needn't show every extreme that they name: `passage_home`: each passage id has its own storage row; storage row r lies on bank index r // 256. `candidates`: among the 128 list entries of one device's queries (aligned blocks of 8 queries, in order), at most 12 name passages stored on one bank index; in every block some bank index gets exactly 12, and in each group of 32 consecutive blocks it is the same bank index for all of them.
All inputs are finite; a program needn't handle non-finite values.
Results may differ from a plain program's by a relative error of at most 0.0049.
Values may be sent and summed in bfloat16 or wider, within the bound.
No kernel may reach another device: no remote copies, remote signals or barrier semaphores. Data moves between devices by JAX's collectives and lax.ppermute only.
A program may use at most 128 MiB of HBM per device.

v0:
```python
import jax
import jax.numpy as jnp
from jax import lax
from jax.sharding import PartitionSpec as P


def soft_terms(scores):
    largest = jnp.max(scores, axis=-1, keepdims=True)
    raised = jnp.exp(scores - largest)
    totals = jnp.sum(raised, axis=-1, keepdims=True)
    maxima = largest[..., 0] + jnp.log(totals[..., 0])
    weights = (raised / totals).astype(jnp.bfloat16)
    return (maxima, weights)


def contrast(similarity, positive):
    largest = jnp.max(similarity, axis=1, keepdims=True)
    raised = jnp.exp(similarity - largest)
    totals = jnp.sum(raised, axis=1, keepdims=True)
    picked = jnp.arange(similarity.shape[1], dtype=jnp.int32)[None, :] == positive[:, None]
    losses = (
        largest[:, 0] + jnp.log(totals[:, 0]) - jnp.sum(jnp.where(picked, similarity, 0.0), axis=1)
    )
    coefficients = (raised / totals - picked.astype(jnp.float32)).astype(jnp.bfloat16)
    return (losses, coefficients)


def body(queries, passages, passage_home, candidates, positive):
    shards = lax.axis_size("bank")
    me = lax.axis_index("bank")
    query_rows, query_len, feature_dim = queries.shape
    listed = candidates.shape[1]
    holdings = passages.shape[0]
    tile_len = passages.shape[1]
    entries = query_rows * listed
    capacity = 3 * entries // shards
    group_rows = shards * query_rows
    lists = jnp.concatenate([candidates, positive[:, None]], axis=1)
    lists = lax.all_gather(lists, "bank", axis=0, tiled=True)
    group_candidates = lists[:, :listed]
    group_positive = lists[:, listed]
    group_queries = lax.all_gather(queries, "bank", axis=0, tiled=True)
    storage = passage_home[group_candidates].reshape(shards, entries)
    mine = storage // holdings == me
    position = jnp.cumsum(mine.astype(jnp.int32), axis=1) - 1
    slot_ids = jnp.arange(capacity, dtype=jnp.int32)
    hit = mine[:, None, :] & (position[:, None, :] == slot_ids[None, :, None])
    valid = jnp.any(hit, axis=2)
    entry_ids = jnp.arange(entries, dtype=jnp.int32)
    entry = jnp.sum(jnp.where(hit, entry_ids[None, None, :], 0), axis=2)
    local_slot = jnp.sum(jnp.where(hit, (storage % holdings)[:, None, :], 0), axis=2)
    source = jnp.arange(shards, dtype=jnp.int32)[:, None]
    query_index = (source * query_rows + entry // listed).reshape(-1)
    flat_index = (source * entries + entry).reshape(-1)
    valid = valid.reshape(-1)
    local_slot = local_slot.reshape(-1)
    passage_tiles = passages[local_slot]
    query_tiles = group_queries[query_index]
    scores = jnp.einsum(
        "sid,sjd->sij", query_tiles, passage_tiles, preferred_element_type=jnp.float32
    )
    maxima, weights = soft_terms(scores)
    token_basis = jnp.einsum(
        "sij,sjd->sid", weights, passage_tiles, preferred_element_type=jnp.float32
    ).astype(jnp.bfloat16)
    slot_similarity = jnp.sum(maxima, axis=1)
    place = flat_index[:, None] == jnp.arange(group_rows * listed, dtype=jnp.int32)[None, :]
    place = place & valid[:, None]
    similarity = jnp.sum(jnp.where(place, slot_similarity[:, None], 0.0), axis=0)
    similarity = lax.psum(similarity, "bank").reshape(group_rows, listed)
    losses, coefficients = contrast(similarity, group_positive)
    slot_coefficient = jnp.where(
        valid, coefficients.reshape(-1)[flat_index], jnp.zeros((), jnp.bfloat16)
    )
    owner = query_index[:, None] == jnp.arange(group_rows, dtype=jnp.int32)[None, :]
    spread = jnp.where(owner, slot_coefficient[:, None], jnp.zeros((), jnp.bfloat16))
    partial = jnp.einsum(
        "sq,sd->qd",
        spread,
        token_basis.reshape(-1, query_len * feature_dim),
        preferred_element_type=jnp.float32,
    )
    gradient = lax.psum_scatter(partial, "bank", scatter_dimension=0, tiled=True)
    own_losses = lax.dynamic_slice_in_dim(losses, me * query_rows, query_rows)
    return (own_losses, gradient.reshape(query_rows, query_len, feature_dim))


def solution(mesh):
    return jax.shard_map(
        body,
        mesh=mesh,
        in_specs=(
            P(("query", "bank"), None, None),
            P("bank", None, None),
            P(),
            P(("query", "bank"), None),
            P(("query", "bank")),
        ),
        out_specs=(P(("query", "bank")), P(("query", "bank"), None, None)),
        check_vma=False,
    )
```

profile of v0, /device:TPU:4, one launch (start us, length us, event | category | flops | bytes accessed | tf_op | source)
XLA Modules:
  0.0 502.4 jit_solution(9782047059398808998)
XLA Ops:
  7.2 0.0 copy-start
  7.2 0.0 all-gather.2.cloned.1.call-start
  7.2 0.7 all-gather.2.cloned.1.call-update
  7.9 0.0 reduce-scatter.2.cloned.1.call-start
  8.0 0.7 copy.13
  8.7 0.8 pad_add_fusion
  9.5 46.7 %all_gather.6 = s32[256,17]{1,0:T(8,128)S(1)} all-gather(s32[8,17]{1,0:T(8,128)S(1)} %pad_add_fusion), channel_id=1, replica_groups=mesh['query'=8,'bank'=32] {'bank'}, dimensions={0}, use_global_device_ids=true | all-gather | bytes 17952 | tf_op jit(solution)/shard_map/all_gather | solution.py:39
  56.2 0.1 reshape.316
  56.3 0.0 copy-done
  56.3 23.0 %gather_fusion = s32[4096]{0:T(1024)S(1)} fusion(s32[8192]{0:T(1024)S(1)} %copy-done, s32[4096]{0:T(1024)S(1)} %broadcast_clamp_fusion), kind=kCustom, calls=%fused_computation | custom fusion | bytes 49152 | tf_op jit(solution)/shard_map/gather | solution.py:43
  79.4 0.3 reduce_window_sum.11
  79.7 0.5 select_reduce_fusion.1
  80.2 0.1 copy.14
  80.3 0.1 reduce_sum.69
  80.4 0.1 reduce_sum.68
  80.5 0.1 add.142
  80.6 0.1 add.158
  80.7 0.1 add.143
  80.8 0.1 add.147
  80.9 0.1 add.148
  81.0 0.1 add.156
  81.1 0.1 copy.17
  81.2 0.1 reshape.309
  81.3 0.3 fusion.13
  81.6 0.1 copy.15
  81.7 0.1 and.84
  81.8 0.2 slice_reduce_fusion
  82.0 0.1 fusion.14
  82.1 0.1 reshape.313
  82.2 14.4 %gather_fusion.2 = bf16[384,128,128]{2,1,0:T(8,128)(2,1)} fusion(bf16[256,128,128]{2,1,0:T(8,128)(2,1)} %param.6, s32[1024]{0:T(1024)S(1)} %pad_clamp_fusion.1), kind=kCustom, calls=%fused_computation.2 | custom fusion | bytes 25167360 | tf_op jit(solution)/shard_map/gather | solution.py:57
  96.7 0.0 all-gather.2.cloned.1.call-done
  96.7 2.8 gather_fusion.1
  99.6 11.3 %fusion.30 = (f32[384,32]{1,0:T(8,128)S(1)}, f32[384,32,128]{2,1,0:T(8,128)}) fusion(bf16[384,32,128]{2,1,0:T(8,128)(2,1)S(1)} %gather_fusion.1, bf16[384,128,128]{2,1,0:T(8,128)(2,1)} %gather_fusion.2), kind=kOutput, calls=%fused_computation.76 | convolution fusion | flops 404213760 | bytes 22069248 | tf_op jit(solution)/shard_map/sid,sjd->sij/dot_general | solution.py:59
  110.9 0.0 copy-start.1
  110.9 5.8 %fusion.1 = f32[384,32]{1,0:T(8,128)S(1)} fusion(f32[384,32,128]{2,1,0:T(8,128)} %get-tuple-element.21, f32[384,32]{1,0:T(8,128)S(1)} %get-tuple-element.20), kind=kLoop, calls=%fused_computation.9 | loop fusion | flops 3133440 | bytes 6389760 | tf_op jit(solution)/shard_map/reduce_sum | solution.py:10
  116.8 0.2 add_reduce_fusion
  116.9 0.0 copy-done.1
  116.9 7.1 %fusion.8 = bf16[384,32,128]{2,1,0:T(8,128)(2,1)S(1)} fusion(bf16[384,128,128]{2,1,0:T(8,128)(2,1)} %gather_fusion.2, f32[384,32,128]{2,1,0:T(8,128)S(1)} %copy-done.1, f32[384,32]{1,0:T(8,128)S(1)} %fusion.1, f32[384,32]{1,0:T(8,128)S(1)} %get-tuple-element.20), kind=kOutput, calls=%fused_computation.16 | convolution fusion | flops 408944640 | bytes 22118400 | tf_op jit(solution)/shard_map/sij,sjd->sid/dot_general | solution.py:63
  124.1 1.9 select_reduce_fusion
  126.0 140.5 %psum.7 = f32[4096]{0:T(1024)S(1)} all-reduce(f32[4096]{0:T(1024)S(1)} %select_reduce_fusion), channel_id=1, replica_groups=mesh['query'=8,'bank'=32] {'bank'}, use_global_device_ids=true, to_apply=%region_8.9 | all-reduce | flops 4096 | bytes 32768 | tf_op jit(solution)/shard_map/psum | solution.py:70
  266.5 0.1 reshape.310
  266.6 0.1 reduce_max.19
  266.7 0.3 exponential_reduce_fusion
  267.0 0.1 div.63
  267.1 0.1 div.64
  267.2 0.1 sub.51
  267.3 0.1 sub.55
  267.4 2.8 gather_fusion.3
  270.2 3.4 fusion.3
  273.7 0.0 reduce-scatter.2.cloned.1.call-update
  273.7 0.6 dynamic_slice.3
  274.3 219.7 %reduce-scatter.2.cloned.1.call-done = f32[8,4096]{1,0:T(8,128)} async-done(((f32[256,4096]{1,0:T(8,128)}), f32[8,4096]{1,0:T(8,128)}) %reduce-scatter.2.cloned.1.call-update) | async-done | bytes 131088 | tf_op jit(solution)/shard_map/reduce_scatter | solution.py:83
  494.0 1.6 copy.18
  (15 shorter events, 0.2 us)
Async XLA Ops:
  7.2 49.1 %copy-start = (s32[8192]{0:T(1024)S(1)}, s32[8192]{0:T(1024)}, u32[]{:S(2)}) copy-start(s32[8192]{0:T(1024)} %param.7) | copy-start | bytes 98308
  7.2 89.6 %all-gather.2.cloned.1.call-start = ((), (), s32[]{:S(2)}) async-start(), calls=%async_computation.1 | async-start | bytes 2162688 | tf_op jit(solution)/shard_map/all_gather | solution.py:42
  7.9 486.1 %reduce-scatter.2.cloned.1.call-start = ((), (), s32[]{:S(2)}) async-start(), calls=%async_computation.2 | async-start | bytes 4325376 | tf_op jit(solution)/shard_map/reduce_scatter | solution.py:83
  110.9 6.0 %copy-start.1 = (f32[384,32,128]{2,1,0:T(8,128)S(1)}, f32[384,32,128]{2,1,0:T(8,128)}, u32[]{:S(2)}) copy-start(f32[384,32,128]{2,1,0:T(8,128)} %get-tuple-element.21) | copy-start | bytes 18874372
Sparse Core Ops, SparseCore 0:
  10.6 80.7 all-gather.1
  273.8 220.1 reduce-scatter.1
where the time goes:
time: 503 us; the launch traced here: 502 us
  waiting for transfers between devices  220 us (44%)
  blocking collectives  187 us (37%)
  local copies, waits for them, and re-layouts  48.1 us (10%)
  matrix products  21.9 us (4%)
  between operations  14.3 us (3%)
  other arithmetic  10.4 us (2%)
    reduce_scatter x1, waiting for transfers between devices, body(): lax.psum_scatter(partial, 'bank', scatter_dimension=0, tiled=True)  220 us
    psum x1, blocking collectives, body(): similarity = lax.psum(similarity, 'bank').reshape(group_rows, listed)  141 us
    all_gather x1, blocking collectives, body(): lists = lax.all_gather(lists, 'bank', axis=0, tiled=True)  46.7 us
    gather x1, local copies, waits for them, and re-layouts, body(): storage = passage_home[group_candidates].reshape(shards, entries)  23 us
    gather x1, local copies, waits for them, and re-layouts, body(): passage_tiles = passages[local_slot]  14.4 us
    dot_general x1, matrix products, body(): jnp.einsum('sid,sjd->sij', query_tiles, passage_tiles, preferred_element_...  11.3 us
  transfers between devices with their start and end apart: 2, of which 1 were waited for; matrix products, arithmetic and copies ran while one was open for 8% of the time, Pallas kernels for 0%

commit v1 on v0

--- a/solution.py
+++ b/solution.py
@@ -67,7 +67,7 @@
     place = flat_index[:, None] == jnp.arange(group_rows * listed, dtype=jnp.int32)[None, :]
     place = place & valid[:, None]
     similarity = jnp.sum(jnp.where(place, slot_similarity[:, None], 0.0), axis=0)
-    similarity = lax.psum(similarity, "bank").reshape(group_rows, listed)
+    similarity = jnp.sum(lax.all_gather(similarity, "bank"), axis=0).reshape(group_rows, listed)
     losses, coefficients = contrast(similarity, group_positive)
     slot_coefficient = jnp.where(
         valid, coefficients.reshape(-1)[flat_index], jnp.zeros((), jnp.bfloat16)

time: 503 us -> 419 us (0.83)
  blocking collectives: 187 us -> 99.7 us
    psum x1 -> x0, blocking collectives: 141 us -> none  [body(): similarity = lax.psum(similarity, 'bank').reshape(group_rows, listed)]
    all_gather x0 -> x1, blocking collectives: none -> 52.9 us  [body(): lax.all_gather(similarity, 'bank')]
  transfers between devices with their start and end apart: 2 -> 2, of which waited for: 1 -> 1; matrix products, arithmetic and copies ran while one was open for 8% -> 10% of each run, Pallas kernels for 0% -> 0%
where the time goes in v1:
time: 419 us; the launch traced here: 418 us
  waiting for transfers between devices  221 us (53%)
  blocking collectives  99.7 us (24%)
  local copies, waits for them, and re-layouts  50.1 us (12%)
  matrix products  21.9 us (5%)
  between operations  14.3 us (3%)
  other arithmetic  11.5 us (3%)
    reduce_scatter x1, waiting for transfers between devices, body(): lax.psum_scatter(partial, 'bank', scatter_dimension=0, tiled=True)  220 us
    all_gather x1, blocking collectives, body(): lax.all_gather(similarity, 'bank')  52.9 us
    all_gather x1, blocking collectives, body(): lists = lax.all_gather(lists, 'bank', axis=0, tiled=True)  46.7 us
    gather x1, local copies, waits for them, and re-layouts, body(): storage = passage_home[group_candidates].reshape(shards, entries)  23 us
    gather x1, local copies, waits for them, and re-layouts, body(): passage_tiles = passages[local_slot]  14.4 us
    dot_general x1, matrix products, body(): jnp.einsum('sid,sjd->sij', query_tiles, passage_tiles, preferred_element_...  11.3 us
  transfers between devices with their start and end apart: 2, of which 1 were waited for; matrix products, arithmetic and copies ran while one was open for 10% of the time, Pallas kernels for 0%

profile of v1, /device:TPU:4, one launch (start us, length us, event | category | flops | bytes accessed | tf_op | source)
XLA Modules:
  0.0 418.3 jit_solution(3127906398412858952)
XLA Ops:
  7.2 0.0 copy-start
  7.2 0.0 all-gather.3.cloned.1.call-start
  7.2 0.7 all-gather.3.cloned.1.call-update
  7.9 0.0 reduce-scatter.2.cloned.1.call-start
  8.0 0.7 copy.13
  8.7 0.8 pad_add_fusion
  9.5 46.7 %all_gather.12 = s32[256,17]{1,0:T(8,128)S(1)} all-gather(s32[8,17]{1,0:T(8,128)S(1)} %pad_add_fusion), channel_id=1, replica_groups=mesh['query'=8,'bank'=32] {'bank'}, dimensions={0}, use_global_device_ids=true | all-gather | bytes 17952 | tf_op jit(solution)/shard_map/all_gather | solution.py:39
  56.2 0.1 reshape.316
  56.3 0.0 copy-done
  56.3 23.0 %gather_fusion = s32[4096]{0:T(1024)S(1)} fusion(s32[8192]{0:T(1024)S(1)} %copy-done, s32[4096]{0:T(1024)S(1)} %broadcast_clamp_fusion), kind=kCustom, calls=%fused_computation | custom fusion | bytes 49152 | tf_op jit(solution)/shard_map/gather | solution.py:43
  79.4 0.3 reduce_window_sum.11
  79.7 0.5 select_reduce_fusion.1
  80.2 0.1 copy.14
  80.3 0.1 reduce_sum.78
  80.4 0.1 reduce_sum.77
  80.5 0.1 add.140
  80.6 0.1 add.156
  80.7 0.1 add.141
  80.8 0.1 add.145
  80.9 0.1 add.146
  81.0 0.1 add.154
  81.1 0.1 copy.17
  81.2 0.1 reshape.309
  81.3 0.3 fusion.13
  81.6 0.1 copy.15
  81.7 0.1 and.84
  81.8 0.2 slice_reduce_fusion
  82.0 0.1 fusion.14
  82.1 0.1 reshape.313
  82.2 14.4 %gather_fusion.2 = bf16[384,128,128]{2,1,0:T(8,128)(2,1)} fusion(bf16[256,128,128]{2,1,0:T(8,128)(2,1)} %param.6, s32[1024]{0:T(1024)S(1)} %pad_clamp_fusion.1), kind=kCustom, calls=%fused_computation.2 | custom fusion | bytes 25167360 | tf_op jit(solution)/shard_map/gather | solution.py:57
  96.7 0.0 all-gather.3.cloned.1.call-done
  96.7 2.8 gather_fusion.1
  99.6 11.3 %fusion.30 = (f32[384,32]{1,0:T(8,128)S(1)}, f32[384,32,128]{2,1,0:T(8,128)}) fusion(bf16[384,32,128]{2,1,0:T(8,128)(2,1)S(1)} %gather_fusion.1, bf16[384,128,128]{2,1,0:T(8,128)(2,1)} %gather_fusion.2), kind=kOutput, calls=%fused_computation.76 | convolution fusion | flops 404213760 | bytes 22069248 | tf_op jit(solution)/shard_map/sid,sjd->sij/dot_general | solution.py:59
  110.9 0.0 copy-start.1
  110.9 5.8 %fusion.1 = f32[384,32]{1,0:T(8,128)S(1)} fusion(f32[384,32,128]{2,1,0:T(8,128)} %get-tuple-element.21, f32[384,32]{1,0:T(8,128)S(1)} %get-tuple-element.20), kind=kLoop, calls=%fused_computation.9 | loop fusion | flops 3133440 | bytes 6389760 | tf_op jit(solution)/shard_map/reduce_sum | solution.py:10
  116.8 0.2 add_reduce_fusion
  116.9 0.0 copy-done.1
  116.9 7.1 %fusion.8 = bf16[384,32,128]{2,1,0:T(8,128)(2,1)S(1)} fusion(bf16[384,128,128]{2,1,0:T(8,128)(2,1)} %gather_fusion.2, f32[384,32,128]{2,1,0:T(8,128)S(1)} %copy-done.1, f32[384,32]{1,0:T(8,128)S(1)} %fusion.1, f32[384,32]{1,0:T(8,128)S(1)} %get-tuple-element.20), kind=kOutput, calls=%fused_computation.16 | convolution fusion | flops 408944640 | bytes 22118400 | tf_op jit(solution)/shard_map/sij,sjd->sid/dot_general | solution.py:63
  124.1 1.9 select_reduce_fusion
  126.0 52.9 %all-gather = f32[131072]{0:T(1024)} all-gather(f32[4096]{0:T(1024)S(1)} %select_reduce_fusion), channel_id=2, replica_groups=mesh['query'=8,'bank'=32] {'bank'}, dimensions={0}, use_global_device_ids=true | all-gather | bytes 540672 | tf_op jit(solution)/shard_map/all_gather | solution.py:70
  178.9 2.0 reshape.346
  180.9 1.1 reduce_sum.83
  182.0 0.1 reshape.310
  182.1 0.1 reduce_max.19
  182.2 0.3 exponential_reduce_fusion
  182.5 0.1 div.63
  182.6 0.1 div.64
  182.7 0.1 sub.51
  182.8 0.1 sub.55
  182.9 2.8 gather_fusion.3
  185.7 3.4 fusion.3
  189.2 0.0 reduce-scatter.2.cloned.1.call-update
  189.2 0.6 dynamic_slice.3
  189.8 220.1 %reduce-scatter.2.cloned.1.call-done = f32[8,4096]{1,0:T(8,128)} async-done(((f32[256,4096]{1,0:T(8,128)}), f32[8,4096]{1,0:T(8,128)}) %reduce-scatter.2.cloned.1.call-update) | async-done | bytes 131088 | tf_op jit(solution)/shard_map/reduce_scatter | solution.py:83
  409.9 1.6 copy.18
  (15 shorter events, 0.2 us)
Async XLA Ops:
  7.2 49.1 %copy-start = (s32[8192]{0:T(1024)S(1)}, s32[8192]{0:T(1024)}, u32[]{:S(2)}) copy-start(s32[8192]{0:T(1024)} %param.7) | copy-start | bytes 98308
  7.2 89.6 %all-gather.3.cloned.1.call-start = ((), (), s32[]{:S(2)}) async-start(), calls=%async_computation.1 | async-start | bytes 2162688 | tf_op jit(solution)/shard_map/all_gather | solution.py:42
  7.9 402.0 %reduce-scatter.2.cloned.1.call-start = ((), (), s32[]{:S(2)}) async-start(), calls=%async_computation.2 | async-start | bytes 4325376 | tf_op jit(solution)/shard_map/reduce_scatter | solution.py:83
  110.9 6.0 %copy-start.1 = (f32[384,32,128]{2,1,0:T(8,128)S(1)}, f32[384,32,128]{2,1,0:T(8,128)}, u32[]{:S(2)}) copy-start(f32[384,32,128]{2,1,0:T(8,128)} %get-tuple-element.21) | copy-start | bytes 18874372
Sparse Core Ops, SparseCore 0:
  10.6 80.7 all-gather.2
  189.3 220.5 reduce-scatter.1
